TPU v7x, 256 devices: a whole 4x4x8 slice. The times are simulated.
256 devices in a mesh: req: 32 (over x, z), kv: 8 (over y, core).
Axes of the slice: x: 4, y: 4, z: 8, core: 2. Of those that a mesh axis runs over, the one named last changes fastest.
Arguments:
- states: bfloat16 [256, 2560], P(('req', 'kv')), may hold values from -6 to 6
- norm_gain: bfloat16 [2560], replicated, may hold values from 0.099609375 to 1.8984375
- w_query: bfloat16 [2560, 2560], P(None, 'kv'), may hold values from -0.125 to 0.125
- key_projection_weight: bfloat16 [2560, 640], P(None, 'kv'), may hold values from -0.125 to 0.125
- value_projection_weight: bfloat16 [2560, 640], P(None, 'kv'), may hold values from -0.125 to 0.125
- cache_keys: bfloat16 [256, 8, 80, 4096], P('req', 'kv')
- value_cache_slots: bfloat16 [256, 8, 80, 4096], P('req', 'kv'), may hold values from -6 to 6
- lengths: int32 [256], P('req'), may hold values from 1 to 16383, as said below
- write_pos: int32 [256], P('req'), may hold values from 0 to 4095, as said below
- dealing: int32 [256], replicated, may hold values from 0 to 255, each once
Outputs:
- context: bfloat16 [256, 2560], P(('req', 'kv'))
Inputs may be any that keep to these rules, and one draw needn't show every extreme that they name: `lengths`: largest value is reached by some request in every draw. write_pos equals lengths modulo 4096. `dealing`: A permutation of the requests.
All inputs are finite; a program needn't handle non-finite values.
Results may differ from a plain program's by a relative error of at most 0.022.
The roundings to bfloat16 on the way count: a program that leaves them out, or rounds other values in their place, can miss the bound.
Values may be sent and summed in bfloat16 or wider, within the bound.
No kernel may reach another device: no remote copies, remote signals or barrier semaphores. Data moves between devices by JAX's collectives and lax.ppermute only.
A program may use at most 64 MiB of HBM per device.

v0:
```python
import jax
import jax.numpy as jnp
from jax import lax
from jax.sharding import PartitionSpec as P

HEAD_DIMENSION = 80


def apply_rotary(tensor, positions):
    half_width = tensor.shape[-1] // 2
    frequency = 10000.0 ** (-(jnp.arange(half_width, dtype=jnp.float32) * 2.0 / tensor.shape[-1]))
    angles = positions.astype(jnp.float32)[:, None] * frequency[None, :]
    cosine = jnp.cos(angles)[:, None, :]
    sine_part = jnp.sin(angles)[:, None, :]
    front_half = tensor[..., :half_width]
    back_half = tensor[..., half_width:]
    return jnp.concatenate(
        [front_half * cosine - back_half * sine_part, back_half * cosine + front_half * sine_part],
        axis=-1,
    )


def local(
    states,
    norm_gain,
    w_query,
    key_projection_weight,
    value_projection_weight,
    cache_keys,
    value_cache_slots,
    lengths,
    write_pos,
    dealing,
):
    kv_count = lax.axis_size("kv")
    per_device = states.shape[0]
    group_rows = per_device * kv_count
    group_index = lax.axis_index("req")
    kv_index = lax.axis_index("kv")
    req_count = lax.axis_size("req")
    dealt_ids = lax.dynamic_slice_in_dim(dealing, group_index * group_rows, group_rows)
    column_rows = lax.all_gather(states, "req", axis=0, tiled=True)
    column_ids = jnp.arange(req_count, dtype=jnp.int32) * kv_count + kv_index
    pick_in = (dealt_ids[:, None] == column_ids[None, :]).astype(jnp.bfloat16)
    own_part = jnp.dot(pick_in, column_rows, preferred_element_type=jnp.float32).astype(
        jnp.bfloat16
    )
    dealt_rows = lax.psum(own_part, "kv")
    wide_rows = dealt_rows.astype(jnp.float32)
    inv_rms = lax.rsqrt(jnp.mean(wide_rows * wide_rows, axis=1, keepdims=True) + 1e-05)
    normalized_input = (wide_rows * inv_rms * norm_gain.astype(jnp.float32)[None, :]).astype(
        jnp.bfloat16
    )
    head_size = HEAD_DIMENSION
    heads_dev = key_projection_weight.shape[1] // head_size
    queries_per_group = w_query.shape[1] // key_projection_weight.shape[1]
    window_size = cache_keys.shape[3]
    query_vectors = jnp.dot(normalized_input, w_query, preferred_element_type=jnp.float32).reshape(
        group_rows, heads_dev * queries_per_group, head_size
    )
    query_vectors = (
        apply_rotary(query_vectors, lengths)
        .astype(jnp.bfloat16)
        .reshape(group_rows, heads_dev, queries_per_group, head_size)
    )
    fresh_key_rows = jnp.dot(
        normalized_input, key_projection_weight, preferred_element_type=jnp.float32
    ).reshape(group_rows, heads_dev, head_size)
    fresh_key_rows = apply_rotary(fresh_key_rows, lengths).astype(jnp.bfloat16)
    fresh_value_rows = (
        jnp.dot(normalized_input, value_projection_weight, preferred_element_type=jnp.float32)
        .astype(jnp.bfloat16)
        .reshape(group_rows, heads_dev, head_size)
    )
    score_scale = 1.0 / head_size**0.5
    scores = (
        jnp.einsum("rkgh,rkhw->rkgw", query_vectors, cache_keys, preferred_element_type=jnp.float32)
        * score_scale
    )
    own_score = (
        jnp.einsum(
            "rkgh,rkh->rkg", query_vectors, fresh_key_rows, preferred_element_type=jnp.float32
        )
        * score_scale
    )
    slot_ids = lax.broadcasted_iota(jnp.int32, (group_rows, 1, 1, window_size), 3)
    at_write = slot_ids == write_pos[:, None, None, None]
    scores = jnp.where(at_write, own_score[..., None], scores)
    scores = jnp.where(slot_ids <= lengths[:, None, None, None], scores, -jnp.inf)
    row_max = jnp.max(scores, axis=-1, keepdims=True)
    expd = jnp.exp(scores - row_max)
    softmax_weights = (expd / jnp.sum(expd, axis=-1, keepdims=True)).astype(jnp.bfloat16)
    stale_weights = jnp.where(at_write, jnp.zeros((), jnp.bfloat16), softmax_weights)
    fresh_weight = jnp.sum(
        jnp.where(at_write, softmax_weights, jnp.zeros((), jnp.bfloat16)).astype(jnp.float32),
        axis=-1,
    )
    mixed = jnp.einsum(
        "rkgw,rkhw->rkgh", stale_weights, value_cache_slots, preferred_element_type=jnp.float32
    )
    mixed = mixed + fresh_weight[..., None] * fresh_value_rows[:, :, None, :].astype(jnp.float32)
    attended = mixed.reshape(group_rows, heads_dev * queries_per_group * head_size).astype(
        jnp.bfloat16
    )
    group_context = lax.all_gather(attended, "kv", axis=1, tiled=True)
    pick_out = (column_ids[:, None] == dealt_ids[None, :]).astype(jnp.bfloat16)
    routed = jnp.dot(pick_out, group_context, preferred_element_type=jnp.float32).astype(
        jnp.bfloat16
    )
    result = lax.psum_scatter(routed, "req", scatter_dimension=0, tiled=True)
    return result


def solution(mesh):
    in_specs = (
        P(("req", "kv"), None),
        P(),
        P(None, "kv"),
        P(None, "kv"),
        P(None, "kv"),
        P("req", "kv", None, None),
        P("req", "kv", None, None),
        P("req"),
        P("req"),
        P(),
    )
    out_specs = P(("req", "kv"), None)
    return jax.shard_map(local, mesh=mesh, in_specs=in_specs, out_specs=out_specs, check_vma=False)
```

profile of v0, /device:TPU:8, one launch (start us, length us, event | category | flops | bytes accessed | tf_op | source)
XLA Modules:
  0.0 262.5 jit_solution(17877185251697256283)
XLA Ops:
  6.5 0.0 copy-start
  6.5 0.0 all-reduce.3.cloned.1.call-start
  6.6 0.8 convert_element_type.54
  7.3 0.7 iota_compare_fusion
  8.1 0.7 convert_element_type.52
  8.8 0.7 iota_compare_fusion.1
  9.5 52.7 %all-gather = bf16[32,1,2560]{2,1,0:T(2,128)(2,1)S(1)} all-gather(bf16[1,1,2560]{2,1,0:T(2,128)(2,1)} %bitcast.43), channel_id=1, replica_groups=mesh['req'=32,'kv'=8] {'req'}, dimensions={0}, use_global_device_ids=true | all-gather | bytes 168960 | tf_op jit(solution)/shard_map/all_gather | solution.py:42
  62.3 0.8 dynamic_slice.3
  63.0 0.2 convolution_convert_fusion.1
  63.2 21.0 %psum.7 = bf16[8,2560]{1,0:T(8,128)(2,1)S(1)} all-reduce(bf16[8,2560]{1,0:T(8,128)(2,1)S(1)} %convolution_convert_fusion.1), channel_id=1, replica_groups=mesh['req'=32,'kv'=8] {'kv'}, use_global_device_ids=true, to_apply=%region_0.0 | all-reduce | flops 20480 | bytes 81920 | tf_op jit(solution)/shard_map/psum | solution.py:48
  84.2 0.1 fusion.28
  84.4 0.1 multiply_cosine_fusion.1
  84.5 1.3 convolution_bitcast_fusion
  85.7 0.1 fusion.48
  85.9 1.3 fusion.22
  87.1 0.0 copy-done
  87.1 0.5 fusion.52
  87.7 0.1 reshape.241
  87.7 0.1 maximum_bitcast_fusion
  87.8 0.1 subtract_convert_fusion
  87.9 0.2 fusion.43
  88.1 0.0 copy-start.1
  88.1 3.7 %fusion.54 = (f32[8,4]{1,0:T(8,128)S(1)}, f32[8,4,4096]{2,1,0:T(4,128)S(1)}) fusion(bf16[8,1,80,4096]{3,2,1,0:T(8,128)(2,1)} %param.15, f32[8,4]{1,0:T(8,128)S(1)} %broadcast_multiply_fusion, pred[8,4096]{1,0:T(8,128)(4,1)S(1)} %iota_compare_fusion, pred[8,4096]{1,0:T(8,128)(4,1)S(1)} %iota_compare_fusion.1, bf16[8,4,40]{2,1,0:T(4,128)(2,1)S(1)} %get-tuple-element.8, ...), kind=kOutput, calls=%fused_computation.64 | convolution fusion | flops 21641216 | bytes 5838080 | tf_op jit(solution)/shard_map/sub | solution.py:91
  91.8 0.4 convert_reduce_fusion
  92.2 4.0 %fusion.19 = bf16[8,4,80]{2,1,0:T(4,128)(2,1)S(1)} fusion(bf16[8,1,80,4096]{3,2,1,0:T(8,128)(2,1)} %param.16, bf16[8,4,4096]{2,1,0:T(4,128)(2,1)S(1)} %get-tuple-element.6, pred[8,4096]{1,0:T(8,128)(4,1)S(1)} %iota_compare_fusion.1, f32[8,80]{1,0:T(8,128)S(1)} %fusion.22, f32[8,4]{1,0:T(8,128)S(1)} %get-tuple-element.5), kind=kOutput, calls=%fused_computation.13 | convolution fusion | flops 21110272 | bytes 5545600 | tf_op jit(solution)/shard_map/rkgw,rkhw->rkgh/dot_general | solution.py:98
  96.1 0.1 convert_element_type.60
  96.2 13.1 %all-gather.1 = bf16[8,320,8]{1,2,0:T(8,128)(2,1)S(1)} all-gather(bf16[1,320,8]{1,2,0:T(8,128)(2,1)S(1)} %bitcast.42), channel_id=1, replica_groups=mesh['req'=32,'kv'=8] {'kv'}, dimensions={0}, use_global_device_ids=true | all-gather | bytes 46080 | tf_op jit(solution)/shard_map/all_gather | solution.py:105
  109.4 0.1 reshape.248
  109.5 0.9 convolution_convert_fusion
  110.4 0.0 all-reduce.3.cloned.1.call-update
  110.4 0.0 copy-done.1
  110.4 0.7 dynamic-slice
  111.1 142.5 %all-reduce.3.cloned.1.call-done = bf16[32,2560]{1,0:T(8,128)(2,1)} async-done(((bf16[32,2560]{1,0:T(8,128)(2,1)}), bf16[32,2560]{1,0:T(8,128)(2,1)}) %all-reduce.3.cloned.1.call-update) | async-done | bytes 163856
  253.6 2.1 constant_dynamic-slice_fusion
  (5 shorter events, 0.0 us)
Async XLA Ops:
  6.5 80.6 %copy-start = (bf16[2560,320]{0,1:T(8,128)(2,1)S(1)}, bf16[2560,320]{0,1:T(8,128)(2,1)}, u32[]{:S(2)}) copy-start(bf16[2560,320]{0,1:T(8,128)(2,1)} %param.12) | copy-start | bytes 4915204
  6.5 247.0 %all-reduce.3.cloned.1.call-start = ((), (), s32[]{:S(2)}) async-start(), calls=%async_computation | async-start | bytes 327680
  88.1 22.3 %copy-start.1 = (u32[256]{0:T(256)S(1)}, u32[256]{0:T(256)}, u32[]{:S(2)}) copy-start(u32[256]{0:T(256)} %constant.44) | copy-start | bytes 3076
Sparse Core Ops, SparseCore 0:
  110.5 142.9 all-reduce.2
where the time goes:
time: 263 us; the launch traced here: 262 us
  waiting for transfers between devices  143 us (54%)
  blocking collectives  86.9 us (33%)
  between operations  13.5 us (5%)
  matrix products  12 us (5%)
  other arithmetic  3.91 us (1%)
  local copies, waits for them, and re-layouts  3.79 us (1%)
    unnamed x2, waiting for transfers between devices  143 us
    all_gather x1, blocking collectives, local(): column_rows = lax.all_gather(states, 'req', axis=0, tiled=True)  52.7 us
    psum x1, blocking collectives, local(): dealt_rows = lax.psum(own_part, 'kv')  21 us
    all_gather x1, blocking collectives, local(): group_context = lax.all_gather(attended, 'kv', axis=1, tiled=True)  13.1 us
  transfers between devices with their start and end apart: 1, of which 1 were waited for; matrix products, arithmetic and copies ran while one was open for 0% of the time, Pallas kernels for 0%

commit v1 on v0

--- a/solution.py
+++ b/solution.py
@@ -45,7 +45,11 @@
     own_part = jnp.dot(pick_in, column_rows, preferred_element_type=jnp.float32).astype(
         jnp.bfloat16
     )
-    dealt_rows = lax.psum(own_part, "kv")
+    dealt_rows = own_part
+    for hop in (1, 2, 4):
+        dealt_rows = dealt_rows + lax.ppermute(
+            dealt_rows, "kv", [(dev, dev ^ hop) for dev in range(8)]
+        )
     wide_rows = dealt_rows.astype(jnp.float32)
     inv_rms = lax.rsqrt(jnp.mean(wide_rows * wide_rows, axis=1, keepdims=True) + 1e-05)
     normalized_input = (wide_rows * inv_rms * norm_gain.astype(jnp.float32)[None, :]).astype(

time: 263 us -> 249 us (0.947)
  blocking collectives: 86.9 us -> 65.9 us
  starting transfers between devices: 0.01 us -> 3.01 us
  waiting for transfers between devices: 143 us -> 146 us
    psum x1 -> x0, blocking collectives: 21 us -> none  [local(): dealt_rows = lax.psum(own_part, 'kv')]
    ppermute x0 -> x3, waiting for transfers between devices: none -> 5.29 us  [local(): lax.ppermute(dealt_rows, 'kv', [(dev, dev ^ hop) for dev in range(8)])]
    ppermute x0 -> x3, starting transfers between devices: none -> 3.01 us  [local(): lax.ppermute(dealt_rows, 'kv', [(dev, dev ^ hop) for dev in range(8)])]
  transfers between devices with their start and end apart: 1 -> 4, of which waited for: 1 -> 3; matrix products, arithmetic and copies ran while one was open for 0% -> 1% of each run, Pallas kernels for 0% -> 0%
where the time goes in v1:
time: 249 us; the launch traced here: 248 us
  waiting for transfers between devices  146 us (59%)
  blocking collectives  65.9 us (26%)
  between operations  13.5 us (5%)
  matrix products  11.9 us (5%)
  other arithmetic  3.89 us (2%)
  local copies, waits for them, and re-layouts  3.78 us (2%)
  starting transfers between devices  3.01 us (1%)
    unnamed x2, waiting for transfers between devices  141 us
    all_gather x1, blocking collectives, local(): column_rows = lax.all_gather(states, 'req', axis=0, tiled=True)  52.8 us
    all_gather x1, blocking collectives, local(): group_context = lax.all_gather(attended, 'kv', axis=1, tiled=True)  13 us
    ppermute x3, waiting for transfers between devices, local(): lax.ppermute(dealt_rows, 'kv', [(dev, dev ^ hop) for dev in range(8)])  5.29 us
  transfers between devices with their start and end apart: 4, of which 3 were waited for; matrix products, arithmetic and copies ran while one was open for 1% of the time, Pallas kernels for 0%

profile of v1, /device:TPU:8, one launch (start us, length us, event | category | flops | bytes accessed | tf_op | source)
XLA Modules:
  0.0 248.3 jit_solution(791129896298751872)
XLA Ops:
  6.5 0.0 copy-start
  6.5 0.0 all-reduce.3.cloned.1.call-start
  6.5 52.8 %all-gather = bf16[32,1,2560]{2,1,0:T(2,128)(2,1)S(1)} all-gather(bf16[1,1,2560]{2,1,0:T(2,128)(2,1)} %bitcast.46), channel_id=1, replica_groups=mesh['req'=32,'kv'=8] {'req'}, dimensions={0}, use_global_device_ids=true | all-gather | bytes 168960 | tf_op jit(solution)/shard_map/all_gather | solution.py:42
  59.4 0.8 dynamic_slice.3
  60.1 0.2 convolution_convert_fusion.1
  60.3 0.1 collective-permute-start
  60.4 0.7 iota_compare_fusion.1
  61.2 0.7 iota_compare_fusion
  61.9 0.0 collective-permute-done
  62.0 0.5 collective-permute-start.1
  62.5 0.7 convert_element_type.54
  63.2 2.9 %collective-permute-done.1 = bf16[8,2560]{1,0:T(8,128)(2,1)S(1)} collective-permute-done((bf16[8,2560]{1,0:T(8,128)(2,1)S(1)}, bf16[8,2560]{1,0:T(8,128)(2,1)S(1)}, u32[]{:S(2)}, u32[]{:S(2)}) %collective-permute-start.1) | collective-permute-done | bytes 40992 | tf_op jit(solution)/shard_map/ppermute | solution.py:50
  66.1 2.4 collective-permute-start.2
  68.5 0.1 multiply_cosine_fusion.1
  68.6 0.7 convert_element_type.52
  69.3 2.4 collective-permute-done.2
  71.7 0.1 fusion.28
  71.8 0.1 fusion.30
  71.9 1.2 fusion.22
  73.1 1.2 convolution_bitcast_fusion
  74.3 0.0 copy-done
  74.3 0.6 fusion.53
  74.9 0.1 fusion.48
  75.0 0.1 reshape.241
  75.1 0.1 maximum_bitcast_fusion
  75.2 0.1 subtract_convert_fusion
  75.2 0.2 fusion.43
  75.5 0.0 copy-start.1
  75.5 3.7 %fusion.50 = (f32[8,4]{1,0:T(8,128)S(1)}, f32[8,4,4096]{2,1,0:T(4,128)S(1)}) fusion(bf16[8,1,80,4096]{3,2,1,0:T(8,128)(2,1)} %param.15, f32[8,4]{1,0:T(8,128)S(1)} %broadcast_multiply_fusion, pred[8,4096]{1,0:T(8,128)(4,1)S(1)} %iota_compare_fusion, pred[8,4096]{1,0:T(8,128)(4,1)S(1)} %iota_compare_fusion.1, bf16[8,4,40]{2,1,0:T(4,128)(2,1)S(1)} %get-tuple-element.8, ...), kind=kOutput, calls=%fused_computation.63 | convolution fusion | flops 21641216 | bytes 5838080 | tf_op jit(solution)/shard_map/sub | solution.py:95
  79.1 0.4 convert_reduce_fusion
  79.5 4.0 %fusion.19 = bf16[8,4,80]{2,1,0:T(4,128)(2,1)S(1)} fusion(bf16[8,1,80,4096]{3,2,1,0:T(8,128)(2,1)} %param.16, bf16[8,4,4096]{2,1,0:T(4,128)(2,1)S(1)} %get-tuple-element.6, pred[8,4096]{1,0:T(8,128)(4,1)S(1)} %iota_compare_fusion.1, f32[8,80]{1,0:T(8,128)S(1)} %fusion.22, f32[8,4]{1,0:T(8,128)S(1)} %get-tuple-element.5), kind=kOutput, calls=%fused_computation.13 | convolution fusion | flops 21110272 | bytes 5545600 | tf_op jit(solution)/shard_map/rkgw,rkhw->rkgh/dot_general | solution.py:102
  83.5 0.1 convert_element_type.60
  83.6 13.0 %all-gather.1 = bf16[8,320,8]{1,2,0:T(8,128)(2,1)S(1)} all-gather(bf16[1,320,8]{1,2,0:T(8,128)(2,1)S(1)} %bitcast.45), channel_id=1, replica_groups=mesh['req'=32,'kv'=8] {'kv'}, dimensions={0}, use_global_device_ids=true | all-gather | bytes 46080 | tf_op jit(solution)/shard_map/all_gather | solution.py:109
  96.6 0.1 reshape.248
  96.7 0.9 convolution_convert_fusion
  97.6 0.0 all-reduce.3.cloned.1.call-update
  97.6 0.0 copy-done.1
  97.6 0.7 dynamic-slice
  98.3 141.1 %all-reduce.3.cloned.1.call-done = bf16[32,2560]{1,0:T(8,128)(2,1)} async-done(((bf16[32,2560]{1,0:T(8,128)(2,1)}), bf16[32,2560]{1,0:T(8,128)(2,1)}) %all-reduce.3.cloned.1.call-update) | async-done | bytes 163856
  239.4 2.1 constant_dynamic-slice_fusion
  (7 shorter events, 0.1 us)
Async XLA Ops:
  6.5 67.8 %copy-start = (bf16[2560,320]{0,1:T(8,128)(2,1)S(1)}, bf16[2560,320]{0,1:T(8,128)(2,1)}, u32[]{:S(2)}) copy-start(bf16[2560,320]{0,1:T(8,128)(2,1)} %param.12) | copy-start | bytes 4915204
  6.5 232.8 %all-reduce.3.cloned.1.call-start = ((), (), s32[]{:S(2)}) async-start(), calls=%async_computation | async-start | bytes 327680
  60.3 1.6 collective-permute-start
  62.0 4.1 %collective-permute-start.1 = (bf16[8,2560]{1,0:T(8,128)(2,1)S(1)}, bf16[8,2560]{1,0:T(8,128)(2,1)S(1)}, u32[]{:S(2)}, u32[]{:S(2)}) collective-permute-start(bf16[8,2560]{1,0:T(8,128)(2,1)S(1)} %add.49), channel_id=1, source_target_pairs={{0,2},{1,3},{2,0},{3,1},{4,6},{5,7},{6,4},{7,5},{8,10},{9,11},{10,... | collective-permute-start | bytes 122888 | tf_op jit(solution)/shard_map/ppermute | solution.py:50
  66.1 5.6 %collective-permute-start.2 = (bf16[8,2560]{1,0:T(8,128)(2,1)S(1)}, bf16[8,2560]{1,0:T(8,128)(2,1)S(1)}, u32[]{:S(2)}, u32[]{:S(2)}) collective-permute-start(bf16[8,2560]{1,0:T(8,128)(2,1)S(1)} %add.50), channel_id=1, source_target_pairs={{0,4},{1,5},{2,6},{3,7},{4,0},{5,1},{6,2},{7,3},{8,12},{9,13},{10,... | collective-permute-start | bytes 122888 | tf_op jit(solution)/shard_map/ppermute | solution.py:50
  75.5 22.2 %copy-start.1 = (u32[256]{0:T(256)S(1)}, u32[256]{0:T(256)}, u32[]{:S(2)}) copy-start(u32[256]{0:T(256)} %constant.44) | copy-start | bytes 3076
Sparse Core Ops, SparseCore 0:
  97.7 141.6 all-reduce.2
